TPU v7x, 256 devices: a whole 4x4x8 slice. The times are simulated.
256 devices in a mesh: dp: 4 (over x), sx: 16 (over y_hi, z), sy: 4 (over y_lo, core).
Axes of the slice: x: 4, y: 4 (y_hi: 2, y_lo: 2; y = y_hi * 2 + y_lo), z: 8, core: 2. Of those that a mesh axis runs over, the one named last changes fastest.
Arguments:
- volume: bfloat16 [4, 256, 64, 32, 128], P('dp', 'sx', 'sy'), may hold values from -6 to 6
- block_active: int32 [4, 16, 4, 2], P('dp', 'sx', 'sy'), may hold values from 0 to 1, as said below
- weight: bfloat16 [3, 3, 3, 128, 128], replicated, may hold values from -0.109375 to 0.109375
- bias: float32 [128], replicated, may hold values from -3 to 3
- cotangent: bfloat16 [4, 256, 64, 32, 128], P('dp', 'sx', 'sy'), may hold values from -0.00390625 to 0.00390625
Outputs:
- activated: bfloat16 [4, 256, 64, 32, 128], P('dp', 'sx', 'sy')
- grad_weight: float32 [3, 3, 3, 128, 128], replicated
- grad_bias: float32 [128], replicated
Inputs may be any that keep to these rules, and one draw needn't show every extreme that they name: `block_active`: every tile of 2 blocks along depth (one value of the first three indices) has at least one active block; the number of active blocks of a tile is drawn evenly from 1 to 2.
All inputs are finite; a program needn't handle non-finite values.
Results may differ from a plain program's by a relative error of at most 0.006.
Values may be sent and summed in bfloat16 or wider, within the bound.
No kernel may reach another device: no remote copies, remote signals or barrier semaphores. Data moves between devices by JAX's collectives and lax.ppermute only.
A program may use at most 64 MiB of HBM per device.

v0:
```python
import jax
import jax.numpy as jnp
from jax import lax
from jax.sharding import PartitionSpec as P


def with_halo(block, sides, width):
    for axis, dim in sides:
        count = lax.axis_size(axis)
        forward = [(i, i + 1) for i in range(count - 1)]
        backward = [(target, source) for source, target in forward]
        low = lax.ppermute(
            lax.slice_in_dim(block, block.shape[dim] - width, None, axis=dim), axis, forward
        )
        high = lax.ppermute(lax.slice_in_dim(block, 0, width, axis=dim), axis, backward)
        block = jnp.concatenate([low, block, high], axis=dim)
    return block


def layer_work(slab, cot_piece, vox_mask, weight, bias):
    pre = (
        lax.conv_general_dilated(
            slab,
            weight,
            (1, 1, 1),
            "VALID",
            dimension_numbers=("NDHWC", "DHWIO", "NDHWC"),
            preferred_element_type=jnp.float32,
        )
        + bias
    )
    sig = jax.nn.sigmoid(pre)
    out = (pre * sig * vox_mask).astype(jnp.bfloat16)
    dpre = (cot_piece.astype(jnp.float32) * sig * (1.0 + pre * (1.0 - sig)) * vox_mask).astype(
        jnp.bfloat16
    )
    span_x = cot_piece.shape[1]
    span_y = cot_piece.shape[2]
    span_z = cot_piece.shape[3]
    channels = cot_piece.shape[4]
    grads = []
    for a in range(3):
        for b in range(3):
            for c in range(3):
                piece = slab[:, a : a + span_x, b : b + span_y, c : c + span_z, :]
                grads.append(
                    lax.dot_general(
                        piece,
                        dpre,
                        (((0, 1, 2, 3), (0, 1, 2, 3)), ((), ())),
                        preferred_element_type=jnp.float32,
                    )
                )
    grad_w = jnp.stack(grads).reshape(3, 3, 3, channels, channels)
    grad_b = jnp.sum(dpre.astype(jnp.float32), axis=(0, 1, 2, 3))
    return (out, grad_w, grad_b)


def local(volume, block_active, weight, bias, cotangent):
    depth = volume.shape[3]
    blocks = block_active.shape[3]
    edge = depth // blocks
    vox_mask = jnp.repeat(block_active, edge, axis=3)[..., None].astype(jnp.float32)
    masked = volume * vox_mask.astype(jnp.bfloat16)
    padded = with_halo(masked, (("sx", 1), ("sy", 2)), 1)
    padded = jnp.pad(padded, ((0, 0), (0, 0), (0, 0), (1, 1), (0, 0)))
    activated, grad_w, grad_b = layer_work(padded, cotangent, vox_mask, weight, bias)
    grad_w, grad_b = lax.psum((grad_w, grad_b), ("dp", "sx", "sy"))
    return (activated, grad_w, grad_b)


def solution(mesh):
    placed = (
        P("dp", "sx", "sy", None, None),
        P("dp", "sx", "sy", None),
        P(),
        P(),
        P("dp", "sx", "sy", None, None),
    )
    return jax.shard_map(
        local,
        mesh=mesh,
        in_specs=placed,
        out_specs=(P("dp", "sx", "sy", None, None), P(), P()),
        check_vma=False,
    )
```

profile of v0, /device:TPU:1, one launch (start us, length us, event | category | flops | bytes accessed | tf_op | source)
XLA Modules:
  0.0 366.7 jit_solution(1537881732760088454)
XLA Ops:
  7.2 0.0 copy-start
  7.2 0.0 all-reduce.3.cloned.1.call-start
  7.2 0.7 convert_bitcast_fusion
  8.0 0.1 broadcast_in_dim.4
  8.0 0.1 convert_element_type.42
  8.1 1.8 broadcast_multiply_fusion
  9.9 4.4 %collective-permute-start = (bf16[1,1,16,32,128]{4,3,2,1,0:T(8,128)(2,1)S(1)}, bf16[1,1,16,32,128]{4,3,2,1,0:T(8,128)(2,1)S(1)}, u32[]{:S(2)}, u32[]{:S(2)}) collective-permute-start(bf16[1,1,16,32,128]{4,3,2,1,0:T(8,128)(2,1)S(1)} %get-tuple-element.15), channel_id=1, source_target_pairs={{0,4},{4,8},{8,12},{12,16},{16,20},{20,24},{24,28},{28,32},{32,36}... | collective-permute-start | bytes 393224 | tf_op jit(solution)/shard_map/ppermute | solution.py:12
  14.3 1.3 collective-permute-start.1
  15.6 0.9 collective-permute-done
  16.5 4.2 %collective-permute-done.1 = bf16[1,1,16,32,128]{4,3,2,1,0:T(8,128)(2,1)S(1)} collective-permute-done((bf16[1,1,16,32,128]{4,3,2,1,0:T(8,128)(2,1)S(1)}, bf16[1,1,16,32,128]{4,3,2,1,0:T(8,128)(2,1)S(1)}, u32[]{:S(2)}, u32[]{:S(2)}) %collective-permute-start.1) | collective-permute-done | bytes 131104 | tf_op jit(solution)/shard_map/ppermute | solution.py:15
  20.7 4.7 %collective-permute-start.2 = (bf16[1,18,1,32,128]{4,3,2,1,0:T(8,128)(2,1)S(1)}, bf16[1,18,1,32,128]{4,3,2,1,0:T(8,128)(2,1)S(1)}, u32[]{:S(2)}, u32[]{:S(2)}) collective-permute-start(bf16[1,18,1,32,128]{4,3,2,1,0:T(8,128)(2,1)S(1)} %get-tuple-element.13), channel_id=1, source_target_pairs={{0,1},{1,2},{2,3},{4,5},{5,6},{6,7},{8,9},{9,10},{10,11},{12,13},{... | collective-permute-start | bytes 442376 | tf_op jit(solution)/shard_map/ppermute | solution.py:12
  25.4 1.9 collective-permute-start.3
  27.4 0.2 collective-permute-done.2
  27.5 4.4 %collective-permute-done.3 = bf16[1,18,1,32,128]{4,3,2,1,0:T(8,128)(2,1)S(1)} collective-permute-done((bf16[1,18,1,32,128]{4,3,2,1,0:T(8,128)(2,1)S(1)}, bf16[1,18,1,32,128]{4,3,2,1,0:T(8,128)(2,1)S(1)}, u32[]{:S(2)}, u32[]{:S(2)}) %collective-permute-start.3) | collective-permute-done | bytes 147488 | tf_op jit(solution)/shard_map/ppermute | solution.py:15
  31.9 0.5 fusion.277
  32.5 1.3 copy.70
  33.8 0.9 pad.5.clone
  34.7 0.4 copy.10
  35.1 0.0 copy-start.5
  35.1 0.3 slice.147
  35.5 0.3 copy-done.4
  35.8 0.0 copy-done.5
  35.8 22.2 %add_divide_fusion = (f32[16,16,8,5,128]{4,2,3,1,0:T(8,128)S(1)}, f32[16,16,8,5,128]{4,2,3,1,0:T(8,128)}, f32[16,16,8,5,128]{4,2,3,1,0:T(8,128)S(1)}) fusion(f32[128]{0:T(128)S(1)} %copy-done.4, pred[8,5]{0,1:T(8,128)(4,1)S(1)} %copy-done.5, bf16[3,3,3,128,128]{4,3,2,1,0:T(8,128)(2,1)S(1)} %copy-done, bf16[18,18,1,7,2,128]{5,3,4,1,0,2:T(8,128)(2,1)S(1)} %slice.147, ...), kind=kOutput, calls=%fused_computation.3 | convolution fusion | flops 9085427712 | bytes 21092904 | tf_op jit(solution)/shard_map/conv_general_dilated | solution.py:22
  58.1 0.9 copy.13
  59.0 0.9 copy.14
  59.9 0.7 copy-done.2
  60.6 1.9 convert_reduce_fusion
  62.5 0.6 pad_maximum_fusion
  63.1 1.1 fusion.221
  64.2 0.9 pad_maximum_fusion.1
  65.1 0.8 fusion.93
  65.9 1.1 fusion.215
  67.0 1.1 fusion.209
  68.1 0.8 fusion.97
  68.9 1.1 fusion.203
  70.0 1.1 fusion.197
  71.2 0.8 fusion.101
  71.9 1.1 fusion.191
  73.0 1.1 fusion.185
  74.2 0.8 fusion.103
  74.9 1.1 fusion.179
  76.1 1.1 fusion.173
  77.2 1.0 fusion.89
  78.2 1.1 fusion.167
  79.3 1.1 fusion.161
  80.4 0.8 fusion.105
  81.2 1.1 fusion.155
  82.3 1.1 fusion.149
  83.4 0.8 fusion.107
  84.2 1.1 fusion.143
  85.3 1.1 fusion.137
  86.4 0.8 fusion.111
  87.2 1.1 fusion.131
  88.4 1.1 fusion.125
  89.5 1.0 fusion.115
  90.5 1.1 fusion.119
  91.7 1.2 copy-done.3
  92.9 0.0 all-reduce.3.cloned.1.call-update
  92.9 3.4 copy.11
  96.3 0.6 fusion.69
  96.9 1.9 copy.42
  98.7 81.1 %psum.15 = f32[128]{0:T(128)} all-reduce(f32[128]{0:T(128)S(1)} %get-tuple-element.6), channel_id=1, replica_groups=mesh['dp'=4,'sx'=16,'sy'=4] {'dp','sx','sy'}, use_global_device_ids=true, to_apply=%region_2.3 | all-reduce | flops 128 | bytes 1024 | tf_op jit(solution)/shard_map/psum | solution.py:68
  179.8 176.8 %all-reduce.3.cloned.1.call-done = f32[3,3,3,128,128]{4,3,2,1,0:T(8,128)} async-done(((f32[3,3,3,128,128]{4,3,2,1,0:T(8,128)}), f32[3,3,3,128,128]{4,3,2,1,0:T(8,128)}) %all-reduce.3.cloned.1.call-update) | async-done | bytes 1769488 | tf_op jit(solution)/shard_map/psum | solution.py:68
  356.6 2.9 copy.154
  (9 shorter events, 0.1 us)
Async XLA Ops:
  7.2 28.3 %copy-start = (bf16[3,3,3,128,128]{4,3,2,1,0:T(8,128)(2,1)S(1)}, bf16[3,3,3,128,128]{4,3,2,1,0:T(8,128)(2,1)}, u32[]{:S(2)}) copy-start(bf16[3,3,3,128,128]{4,3,2,1,0:T(8,128)(2,1)} %param.7) | copy-start | bytes 2654212
  7.2 349.4 %all-reduce.3.cloned.1.call-start = ((), (), s32[]{:S(2)}) async-start(), calls=%async_computation | async-start | bytes 3538944 | tf_op jit(solution)/shard_map/psum | solution.py:68
  9.9 6.5 %collective-permute-start = (bf16[1,1,16,32,128]{4,3,2,1,0:T(8,128)(2,1)S(1)}, bf16[1,1,16,32,128]{4,3,2,1,0:T(8,128)(2,1)S(1)}, u32[]{:S(2)}, u32[]{:S(2)}) collective-permute-start(bf16[1,1,16,32,128]{4,3,2,1,0:T(8,128)(2,1)S(1)} %get-tuple-element.15), channel_id=1, source_target_pairs={{0,4},{4,8},{8,12},{12,16},{16,20},{20,24},{24,28},{28,32},{32,36}... | collective-permute-start | bytes 393224 | tf_op jit(solution)/shard_map/ppermute | solution.py:12
  14.3 6.4 %collective-permute-start.1 = (bf16[1,1,16,32,128]{4,3,2,1,0:T(8,128)(2,1)S(1)}, bf16[1,1,16,32,128]{4,3,2,1,0:T(8,128)(2,1)S(1)}, u32[]{:S(2)}, u32[]{:S(2)}) collective-permute-start(bf16[1,1,16,32,128]{4,3,2,1,0:T(8,128)(2,1)S(1)} %get-tuple-element.16), channel_id=1, source_target_pairs={{4,0},{8,4},{12,8},{16,12},{20,16},{24,20},{28,24},{32,28},{36,32}... | collective-permute-start | bytes 393224 | tf_op jit(solution)/shard_map/ppermute | solution.py:15
  20.7 6.8 %collective-permute-start.2 = (bf16[1,18,1,32,128]{4,3,2,1,0:T(8,128)(2,1)S(1)}, bf16[1,18,1,32,128]{4,3,2,1,0:T(8,128)(2,1)S(1)}, u32[]{:S(2)}, u32[]{:S(2)}) collective-permute-start(bf16[1,18,1,32,128]{4,3,2,1,0:T(8,128)(2,1)S(1)} %get-tuple-element.13), channel_id=1, source_target_pairs={{0,1},{1,2},{2,3},{4,5},{5,6},{6,7},{8,9},{9,10},{10,11},{12,13},{... | collective-permute-start | bytes 442376 | tf_op jit(solution)/shard_map/ppermute | solution.py:12
  25.4 6.5 %collective-permute-start.3 = (bf16[1,18,1,32,128]{4,3,2,1,0:T(8,128)(2,1)S(1)}, bf16[1,18,1,32,128]{4,3,2,1,0:T(8,128)(2,1)S(1)}, u32[]{:S(2)}, u32[]{:S(2)}) collective-permute-start(bf16[1,18,1,32,128]{4,3,2,1,0:T(8,128)(2,1)S(1)} %get-tuple-element.14), channel_id=1, source_target_pairs={{1,0},{2,1},{3,2},{5,4},{6,5},{7,6},{9,8},{10,9},{11,10},{13,12},{... | collective-permute-start | bytes 442376 | tf_op jit(solution)/shard_map/ppermute | solution.py:15
  35.1 0.7 copy-start.4
  35.1 0.7 copy-start.5
  59.0 1.6 copy-start.2
  91.6 1.2 copy-start.3
  96.8 262.6 %copy-start.1 = (bf16[3,3,3,128,128]{4,3,2,1,0:T(8,128)(2,1)S(1)}, bf16[3,3,3,128,128]{4,3,2,1,0:T(8,128)(2,1)}, u32[]{:S(2)}) copy-start(bf16[3,3,3,128,128]{4,3,2,1,0:T(8,128)(2,1)} %param.7) | copy-start | bytes 2654212
Sparse Core Ops, SparseCore 0:
  93.0 263.5 all-reduce.2
where the time goes:
time: 371 us; the launch traced here: 367 us
  waiting for transfers between devices  186 us (50%)
  blocking collectives  81.1 us (22%)
  matrix products  49.8 us (13%)
  local copies, waits for them, and re-layouts  15.3 us (4%)
  between operations  14.8 us (4%)
  starting transfers between devices  12.3 us (3%)
  other arithmetic  7.05 us (2%)
    psum x1, waiting for transfers between devices, local(): grad_w, grad_b = lax.psum((grad_w, grad_b), ('dp', 'sx', 'sy'))  177 us
    psum x1, blocking collectives, local(): grad_w, grad_b = lax.psum((grad_w, grad_b), ('dp', 'sx', 'sy'))  81.1 us
    dot_general x27, matrix products, layer_work(): lax.dot_general(piece, dpre, (((0, 1, 2, 3), (0, 1, 2, 3)), ((), ())), pr...  27.5 us
    conv_general_dilated x1, matrix products, layer_work(): lax.conv_general_dilated(slab, weight, (1, 1, 1), 'VALID', dimension_numb...  22.2 us
    ppermute x2, starting transfers between devices, with_halo(): lax.ppermute(lax.slice_in_dim(block, block.shape[dim] - width, None, axis...  9.09 us
    ppermute x2, waiting for transfers between devices, with_halo(): lax.ppermute(lax.slice_in_dim(block, 0, width, axis=dim), axis, backward)  8.58 us
    unnamed x15, local copies, waits for them, and re-layouts  8.22 us
  transfers between devices with their start and end apart: 5, of which 5 were waited for; matrix products, arithmetic and copies ran while one was open for 2% of the time, Pallas kernels for 0%

commit v1 on v0

--- a/solution.py
+++ b/solution.py
@@ -1,7 +1,7 @@
 import jax
 import jax.numpy as jnp
 from jax import lax
-from jax.sharding import PartitionSpec as P
+from jax.sharding import Mesh, PartitionSpec as P
 
 
 def with_halo(block, sides, width):
@@ -56,31 +56,70 @@
     return (out, grad_w, grad_b)
 
 
+def group_size(axes):
+    size = 1
+    for axis in axes:
+        size *= lax.axis_size(axis)
+    return size
+
+
+def scatter_sum(flat, axes):
+    parts = lax.all_to_all(flat.reshape(group_size(axes), -1), axes, 0, 0, tiled=True)
+    return parts.sum(0)
+
+
+def gather_back(piece, axes):
+    count = group_size(axes)
+    parts = jnp.broadcast_to(piece[None], (count,) + piece.shape)
+    return lax.all_to_all(parts, axes, 0, 0, tiled=True).reshape(-1)
+
+
+STAGES = (("yh", "yl", "c"), ("x", "z"))
+
+
+def reduce_grads(grad_w, grad_b):
+    total = grad_w.size + grad_b.size
+    devices = group_size(sum(STAGES, ()))
+    padded = -(-total // devices) * devices
+    flat = jnp.concatenate(
+        [grad_w.reshape(-1), grad_b, jnp.zeros((padded - total,), jnp.float32)]
+    )
+    for axes in STAGES:
+        flat = scatter_sum(flat, axes)
+    for axes in reversed(STAGES):
+        flat = gather_back(flat, axes)
+    return flat[: grad_w.size].reshape(grad_w.shape), flat[grad_w.size : total]
+
+
 def local(volume, block_active, weight, bias, cotangent):
     depth = volume.shape[3]
     blocks = block_active.shape[3]
     edge = depth // blocks
     vox_mask = jnp.repeat(block_active, edge, axis=3)[..., None].astype(jnp.float32)
     masked = volume * vox_mask.astype(jnp.bfloat16)
-    padded = with_halo(masked, (("sx", 1), ("sy", 2)), 1)
+    padded = with_halo(masked, ((("yh", "z"), 1), (("yl", "c"), 2)), 1)
     padded = jnp.pad(padded, ((0, 0), (0, 0), (0, 0), (1, 1), (0, 0)))
     activated, grad_w, grad_b = layer_work(padded, cotangent, vox_mask, weight, bias)
-    grad_w, grad_b = lax.psum((grad_w, grad_b), ("dp", "sx", "sy"))
+    grad_w, grad_b = reduce_grads(grad_w, grad_b)
     return (activated, grad_w, grad_b)
 
 
 def solution(mesh):
+    dp, sx, sy = (mesh.shape[name] for name in ("dp", "sx", "sy"))
+    shape = (dp, 2, sx // 2, sy // 2, 2)
+    physical = Mesh(mesh.devices.reshape(shape), ("x", "yh", "z", "yl", "c"))
+    tiles = ("x", ("yh", "z"), ("yl", "c"))
     placed = (
-        P("dp", "sx", "sy", None, None),
-        P("dp", "sx", "sy", None),
+        P(*tiles, None, None),
+        P(*tiles, None),
         P(),
         P(),
-        P("dp", "sx", "sy", None, None),
+        P(*tiles, None, None),
     )
     return jax.shard_map(
         local,
-        mesh=mesh,
+        mesh=physical,
         in_specs=placed,
-        out_specs=(P("dp", "sx", "sy", None, None), P(), P()),
+        out_specs=(P(*tiles, None, None), P(), P()),
         check_vma=False,
     )

time: 371 us -> 199 us (0.54)
  waiting for transfers between devices: 186 us -> 26.5 us
  blocking collectives: 81.1 us -> 62 us
  between operations: 14.8 us -> 1.3 us
  local copies, waits for them, and re-layouts: 15.3 us -> 22.5 us
  starting transfers between devices: 12.3 us -> 19.4 us
  other arithmetic: 7.05 us -> 13.7 us
    psum x1 -> x0, waiting for transfers between devices: 177 us -> none  [local(): grad_w, grad_b = lax.psum((grad_w, grad_b), ('dp', 'sx', 'sy'))]
    psum x1 -> x0, blocking collectives: 81.1 us -> none  [local(): grad_w, grad_b = lax.psum((grad_w, grad_b), ('dp', 'sx', 'sy'))]
    all_to_all x0 -> x3, blocking collectives: none -> 62 us  [the longest x2 47 us: scatter_sum(): lax.all_to_all(flat.reshape(group_size(axes), -1), axes, 0, 0, tiled=True)]
    all_to_all x0 -> x1, waiting for transfers between devices: none -> 16.9 us  [gather_back(): return lax.all_to_all(parts, axes, 0, 0, tiled=True).reshape(-1)]
    all_to_all x0 -> x1, starting transfers between devices: none -> 7.07 us  [gather_back(): return lax.all_to_all(parts, axes, 0, 0, tiled=True).reshape(-1)]
    all_to_all x0 -> x2, other arithmetic: none -> 5.05 us  [gather_back(): return lax.all_to_all(parts, axes, 0, 0, tiled=True).reshape(-1)]
    unnamed x15 -> x12, local copies, waits for them, and re-layouts: 8.22 us -> 4.15 us
    slice x0 -> x2, local copies, waits for them, and re-layouts: none -> 3.99 us  [reduce_grads(): return (flat[:grad_w.size].reshape(grad_w.shape), flat[grad_w.size:total])]
  transfers between devices with their start and end apart: 5 -> 5, of which waited for: 5 -> 5; matrix products, arithmetic and copies ran while one was open for 2% -> 3% of each run, Pallas kernels for 0% -> 0%
where the time goes in v1:
time: 199 us; the launch traced here: 195 us
  blocking collectives  62 us (31%)
  matrix products  49.6 us (25%)
  waiting for transfers between devices  26.5 us (13%)
  local copies, waits for them, and re-layouts  22.5 us (11%)
  starting transfers between devices  19.4 us (10%)
  other arithmetic  13.7 us (7%)
    all_to_all x2, blocking collectives, scatter_sum(): lax.all_to_all(flat.reshape(group_size(axes), -1), axes, 0, 0, tiled=True)  47 us
    dot_general x27, matrix products, layer_work(): lax.dot_general(piece, dpre, (((0, 1, 2, 3), (0, 1, 2, 3)), ((), ())), pr...  27.4 us
    conv_general_dilated x1, matrix products, layer_work(): lax.conv_general_dilated(slab, weight, (1, 1, 1), 'VALID', dimension_numb...  22.1 us
    all_to_all x1, waiting for transfers between devices, gather_back(): return lax.all_to_all(parts, axes, 0, 0, tiled=True).reshape(-1)  16.9 us
    all_to_all x1, blocking collectives, gather_back(): return lax.all_to_all(parts, axes, 0, 0, tiled=True).reshape(-1)  15.1 us
    ppermute x2, starting transfers between devices, with_halo(): lax.ppermute(lax.slice_in_dim(block, block.shape[dim] - width, None, axis...  9.09 us
    ppermute x2, waiting for transfers between devices, with_halo(): lax.ppermute(lax.slice_in_dim(block, 0, width, axis=dim), axis, backward)  8.58 us
    all_to_all x1, starting transfers between devices, gather_back(): return lax.all_to_all(parts, axes, 0, 0, tiled=True).reshape(-1)  7.07 us
  transfers between devices with their start and end apart: 5, of which 5 were waited for; matrix products, arithmetic and copies ran while one was open for 3% of the time, Pallas kernels for 0%

profile of v1, /device:TPU:1, one launch (start us, length us, event | category | flops | bytes accessed | tf_op | source)
XLA Modules:
  0.0 194.9 jit_solution(3297994382701021138)
XLA Ops:
  0.6 0.7 convert_bitcast_fusion
  1.5 1.8 broadcast_multiply_fusion
  3.4 4.4 %collective-permute-start = (bf16[1,1,16,32,128]{4,3,2,1,0:T(8,128)(2,1)S(1)}, bf16[1,1,16,32,128]{4,3,2,1,0:T(8,128)(2,1)S(1)}, u32[]{:S(2)}, u32[]{:S(2)}) collective-permute-start(bf16[1,1,16,32,128]{4,3,2,1,0:T(8,128)(2,1)S(1)} %get-tuple-element.21), channel_id=1, source_target_pairs={{0,4},{4,8},{8,12},{12,16},{16,20},{20,24},{24,28},{28,32},{32,36}... | collective-permute-start | bytes 393224 | tf_op jit(solution)/shard_map/ppermute | solution.py:12
  7.8 1.3 collective-permute-start.1
  9.1 0.9 collective-permute-done
  9.9 4.2 %collective-permute-done.1 = bf16[1,1,16,32,128]{4,3,2,1,0:T(8,128)(2,1)S(1)} collective-permute-done((bf16[1,1,16,32,128]{4,3,2,1,0:T(8,128)(2,1)S(1)}, bf16[1,1,16,32,128]{4,3,2,1,0:T(8,128)(2,1)S(1)}, u32[]{:S(2)}, u32[]{:S(2)}) %collective-permute-start.1) | collective-permute-done | bytes 131104 | tf_op jit(solution)/shard_map/ppermute | solution.py:15
  14.1 4.7 %collective-permute-start.2 = (bf16[1,18,1,32,128]{4,3,2,1,0:T(8,128)(2,1)S(1)}, bf16[1,18,1,32,128]{4,3,2,1,0:T(8,128)(2,1)S(1)}, u32[]{:S(2)}, u32[]{:S(2)}) collective-permute-start(bf16[1,18,1,32,128]{4,3,2,1,0:T(8,128)(2,1)S(1)} %get-tuple-element.19), channel_id=1, source_target_pairs={{0,1},{1,2},{2,3},{4,5},{5,6},{6,7},{8,9},{9,10},{10,11},{12,13},{... | collective-permute-start | bytes 442376 | tf_op jit(solution)/shard_map/ppermute | solution.py:12
  18.9 1.9 collective-permute-start.3
  21.0 4.4 %collective-permute-done.3 = bf16[1,18,1,32,128]{4,3,2,1,0:T(8,128)(2,1)S(1)} collective-permute-done((bf16[1,18,1,32,128]{4,3,2,1,0:T(8,128)(2,1)S(1)}, bf16[1,18,1,32,128]{4,3,2,1,0:T(8,128)(2,1)S(1)}, u32[]{:S(2)}, u32[]{:S(2)}) %collective-permute-start.3) | collective-permute-done | bytes 147488 | tf_op jit(solution)/shard_map/ppermute | solution.py:15
  25.3 0.5 fusion.277
  25.9 1.3 copy.144
  27.2 0.9 pad.5.clone
  28.1 0.4 copy.80
  28.6 0.3 slice.155
  29.3 22.1 %add_divide_fusion = (f32[16,16,8,5,128]{4,2,3,1,0:T(8,128)S(1)}, f32[16,16,8,5,128]{4,2,3,1,0:T(8,128)}, f32[16,16,8,5,128]{4,2,3,1,0:T(8,128)S(1)}) fusion(f32[128]{0:T(128)S(1)} %copy-done.3, pred[8,5]{0,1:T(8,128)(4,1)S(1)} %copy-done.4, bf16[3,3,3,128,128]{4,3,2,1,0:T(8,128)(2,1)S(1)} %copy-done, bf16[18,18,1,7,2,128]{5,3,4,1,0,2:T(8,128)(2,1)S(1)} %slice.155, ...), kind=kOutput, calls=%fused_computation.3 | convolution fusion | flops 9085427712 | bytes 21092904 | tf_op jit(solution)/shard_map/conv_general_dilated | solution.py:22
  51.4 0.9 copy.83
  52.3 0.9 copy.84
  53.3 0.7 copy-done.2
  53.9 1.9 convert_reduce_fusion
  55.9 0.6 pad_maximum_fusion
  56.4 1.1 fusion.221
  57.5 0.9 pad_maximum_fusion.1
  58.4 0.8 fusion.93
  59.2 1.1 fusion.215
  60.3 1.1 fusion.209
  61.4 0.8 fusion.97
  62.2 1.1 fusion.203
  63.4 1.1 fusion.197
  64.5 0.8 fusion.101
  65.2 1.1 fusion.191
  66.4 1.1 fusion.185
  67.5 0.8 fusion.103
  68.3 1.1 fusion.179
  69.4 1.1 fusion.173
  70.5 1.0 fusion.89
  71.5 1.1 fusion.167
  72.6 1.1 fusion.161
  73.7 0.8 fusion.105
  74.5 1.1 fusion.155
  75.6 1.1 fusion.149
  76.7 0.8 fusion.107
  77.5 1.1 fusion.143
  78.6 1.1 fusion.137
  79.7 0.8 fusion.111
  80.5 1.1 fusion.131
  81.7 1.1 fusion.125
  82.8 1.0 fusion.115
  83.8 1.1 fusion.119
  85.0 2.3 %all_to_all.20 = f32[8,1,55328]{2,1,0:T(1,128)S(1)} reshape(f32[442624]{0:T(1024)S(1)} %pad_maximum_fusion.4) | data formatting | bytes 3540992 | tf_op jit(solution)/shard_map/all_to_all | solution.py:67
  87.3 29.1 %all_to_all.30 = f32[8,1,55328]{2,1,0:T(1,128)S(1)} all-to-all(f32[8,1,55328]{2,1,0:T(1,128)S(1)} %all_to_all.20), channel_id=1, replica_groups=mesh['x'=4,'yh'=2,'z'=8,'yl'=2,'c'=2] {'yh','yl','c'}, dimensions={0} | all-to-all | bytes 3540992 | tf_op jit(solution)/shard_map/all_to_all | solution.py:67
  116.4 1.3 reduce_sum.28
  118.1 17.8 %all_to_all.31 = f32[32,1,1729]{2,1,0:T(1,128)S(1)} all-to-all(f32[32,1,1729]{2,1,0:T(1,128)S(1)} %all_to_all.22), channel_id=1, replica_groups=mesh['x'=4,'yh'=2,'z'=8,'yl'=2,'c'=2] {'x','z'}, dimensions={0} | all-to-all | bytes 442624 | tf_op jit(solution)/shard_map/all_to_all | solution.py:67
  136.2 15.1 %all_to_all.32 = f32[32,1,1729]{2,1,0:T(1,128)S(1)} all-to-all(f32[32,1,1729]{2,1,0:T(1,128)S(1)} %broadcast_in_dim.22), channel_id=1, replica_groups=mesh['x'=4,'yh'=2,'z'=8,'yl'=2,'c'=2] {'x','z'}, dimensions={0} | all-to-all | bytes 442624 | tf_op jit(solution)/shard_map/all_to_all | solution.py:74
  151.3 0.5 reduce.2
  152.0 2.2 %broadcast_in_dim.24 = f32[8,1,55328]{2,1,0:T(1,128)} broadcast(f32[55328]{0:T(1024)S(1)} %broadcast_in_dim.23), dimensions={2} | broadcast | bytes 1991808 | tf_op jit(solution)/shard_map/broadcast_in_dim | solution.py:73
  154.2 7.1 %all-to-all-start.3 = ((f32[8,1,55328]{2,1,0:T(1,128)}), f32[8,1,55328]{2,1,0:T(1,128)S(1)}, u32[]{:S(2)}, u32[]{:S(2)}) async-start(f32[8,1,55328]{2,1,0:T(1,128)} %broadcast_in_dim.24), calls=%async_computation.3 | async-start | bytes 3547136 | tf_op jit(solution)/shard_map/all_to_all | solution.py:74
  161.2 3.4 %copy.81 = f32[16,16,8,5,128]{4,1,3,2,0:T(8,128)S(1)} copy(f32[16,16,8,5,128]{4,2,3,1,0:T(8,128)} %get-tuple-element.15) | data formatting | bytes 10485760 | tf_op jit(solution)/shard_map/mul | solution.py:33
  164.6 0.6 fusion.69
  165.2 1.9 copy.114
  167.1 16.9 %all-to-all-done.3 = f32[8,1,55328]{2,1,0:T(1,128)S(1)} async-done(((f32[8,1,55328]{2,1,0:T(1,128)}), f32[8,1,55328]{2,1,0:T(1,128)S(1)}, u32[]{:S(2)}, u32[]{:S(2)}) %all-to-all-start.3) | async-done | bytes 1770528 | tf_op jit(solution)/shard_map/all_to_all | solution.py:74
  184.0 4.5 %reduce.3 = f32[8,55328]{1,0:T(8,128)S(1)} reduce(f32[8,1,55328]{2,1,0:T(1,128)S(1)} %all-to-all-done.3, f32[]{:T(128)} %constant.18), dimensions={1}, to_apply=%all_to_all.25.reduce_sub_computation | reduce | bytes 3540996 | tf_op jit(solution)/shard_map/all_to_all | solution.py:74
  188.5 2.2 %reshape.202 = f32[442624]{0:T(1024)} reshape(f32[8,55328]{1,0:T(8,128)S(1)} %reduce.3) | data formatting | bytes 3540992 | tf_op jit(solution)/shard_map/reshape | solution.py:74
  190.7 2.8 %slice.165 = f32[442368]{0:T(1024)} slice(f32[442624]{0:T(1024)} %reshape.202), slice={[0:442368]} | slice | bytes 3538944 | tf_op jit(solution)/shard_map/slice | solution.py:91
  193.5 1.2 slice.166
  (21 shorter events, 1.6 us)
Async XLA Ops:
  0.6 28.3 %copy-start = (bf16[3,3,3,128,128]{4,3,2,1,0:T(8,128)(2,1)S(1)}, bf16[3,3,3,128,128]{4,3,2,1,0:T(8,128)(2,1)}, u32[]{:S(2)}) copy-start(bf16[3,3,3,128,128]{4,3,2,1,0:T(8,128)(2,1)} %param.7) | copy-start | bytes 2654212
  3.4 6.5 %collective-permute-start = (bf16[1,1,16,32,128]{4,3,2,1,0:T(8,128)(2,1)S(1)}, bf16[1,1,16,32,128]{4,3,2,1,0:T(8,128)(2,1)S(1)}, u32[]{:S(2)}, u32[]{:S(2)}) collective-permute-start(bf16[1,1,16,32,128]{4,3,2,1,0:T(8,128)(2,1)S(1)} %get-tuple-element.21), channel_id=1, source_target_pairs={{0,4},{4,8},{8,12},{12,16},{16,20},{20,24},{24,28},{28,32},{32,36}... | collective-permute-start | bytes 393224 | tf_op jit(solution)/shard_map/ppermute | solution.py:12
  7.8 6.4 %collective-permute-start.1 = (bf16[1,1,16,32,128]{4,3,2,1,0:T(8,128)(2,1)S(1)}, bf16[1,1,16,32,128]{4,3,2,1,0:T(8,128)(2,1)S(1)}, u32[]{:S(2)}, u32[]{:S(2)}) collective-permute-start(bf16[1,1,16,32,128]{4,3,2,1,0:T(8,128)(2,1)S(1)} %get-tuple-element.22), channel_id=1, source_target_pairs={{4,0},{8,4},{12,8},{16,12},{20,16},{24,20},{28,24},{32,28},{36,32}... | collective-permute-start | bytes 393224 | tf_op jit(solution)/shard_map/ppermute | solution.py:15
  14.1 6.8 %collective-permute-start.2 = (bf16[1,18,1,32,128]{4,3,2,1,0:T(8,128)(2,1)S(1)}, bf16[1,18,1,32,128]{4,3,2,1,0:T(8,128)(2,1)S(1)}, u32[]{:S(2)}, u32[]{:S(2)}) collective-permute-start(bf16[1,18,1,32,128]{4,3,2,1,0:T(8,128)(2,1)S(1)} %get-tuple-element.19), channel_id=1, source_target_pairs={{0,1},{1,2},{2,3},{4,5},{5,6},{6,7},{8,9},{9,10},{10,11},{12,13},{... | collective-permute-start | bytes 442376 | tf_op jit(solution)/shard_map/ppermute | solution.py:12
  18.9 6.5 %collective-permute-start.3 = (bf16[1,18,1,32,128]{4,3,2,1,0:T(8,128)(2,1)S(1)}, bf16[1,18,1,32,128]{4,3,2,1,0:T(8,128)(2,1)S(1)}, u32[]{:S(2)}, u32[]{:S(2)}) collective-permute-start(bf16[1,18,1,32,128]{4,3,2,1,0:T(8,128)(2,1)S(1)} %get-tuple-element.20), channel_id=1, source_target_pairs={{1,0},{2,1},{3,2},{5,4},{6,5},{7,6},{9,8},{10,9},{11,10},{13,12},{... | collective-permute-start | bytes 442376 | tf_op jit(solution)/shard_map/ppermute | solution.py:15
  28.6 0.7 copy-start.3
  28.6 0.7 copy-start.4
  52.3 1.6 copy-start.2
  154.2 29.8 %all-to-all-start.3 = ((f32[8,1,55328]{2,1,0:T(1,128)}), f32[8,1,55328]{2,1,0:T(1,128)S(1)}, u32[]{:S(2)}, u32[]{:S(2)}) async-start(f32[8,1,55328]{2,1,0:T(1,128)} %broadcast_in_dim.24), calls=%async_computation.3 | async-start | bytes 3547136 | tf_op jit(solution)/shard_map/all_to_all | solution.py:74
  188.5 6.2 %copy-start.1 = (bf16[3,3,3,128,128]{4,3,2,1,0:T(8,128)(2,1)S(1)}, bf16[3,3,3,128,128]{4,3,2,1,0:T(8,128)(2,1)}, u32[]{:S(2)}) copy-start(bf16[3,3,3,128,128]{4,3,2,1,0:T(8,128)(2,1)} %param.7) | copy-start | bytes 2654212
